TPU v7x, 128 devices: a whole 4x4x4 slice. The times are simulated.
128 devices in a mesh: dp: 4 (over z_hi, core), mp: 32 (over x, y, z_lo).
Axes of the slice: x: 4, y: 4, z: 4 (z_hi: 2, z_lo: 2; z = z_hi * 2 + z_lo), core: 2. Of those that a mesh axis runs over, the one named last changes fastest.
Arguments:
- residual_input: bfloat16 [2048, 4608], P(('dp', 'mp')), may hold values from -6 to 6
- before_attention_gain: float32 [4608], replicated, may hold values from 0.25 to 1.75
- after_attention_gain: float32 [4608], replicated, may hold values from 0.25 to 1.75
- before_feedforward_gain: float32 [4608], replicated, may hold values from 0.25 to 1.75
- after_feedforward_gain: float32 [4608], replicated, may hold values from 0.25 to 1.75
- query_weight: bfloat16 [4608, 4096], P(None, 'mp'), may hold values from -0.09375 to 0.09375
- key_value_weight: bfloat16 [4608, 2, 32, 128], P(None, None, 'mp'), as said below
- output_weight: bfloat16 [4096, 4608], P('mp'), may hold values from -0.09375 to 0.09375
- gate_matrix: bfloat16 [4608, 20480], P(None, 'mp'), may hold values from -0.09375 to 0.09375
- up_matrix: bfloat16 [4608, 20480], P(None, 'mp'), may hold values from -0.09375 to 0.09375
- down_matrix: bfloat16 [20480, 4608], P('mp'), may hold values from -0.0390625 to 0.0390625
- key_value_cache: bfloat16 [256, 2, 32, 16, 128], P('dp', None, 'mp'), as said below
- projected_lowrank_left: bfloat16 [64, 4608, 16], P('mp'), may hold values from -0.09375 to 0.09375
- projected_lowrank_right: bfloat16 [64, 16, 3, 32, 128], P(None, None, None, 'mp'), as said below
- result_lowrank_left: bfloat16 [64, 4096, 16], P(None, 'mp'), may hold values from -0.09375 to 0.09375
- result_lowrank_right: bfloat16 [64, 16, 4608], P('mp'), may hold values from -1.5 to 1.5
- token_request: int32 [4, 512], P('dp'), may hold values from 0 to 7, never falling along the last dimension, each value on 1 to 256 neighbouring positions
- lowrank_choice_by_prompt: int32 [4, 8], P('dp'), may hold values from 0 to 63
- adapter_position: int32 [64], replicated, may hold values from 0 to 63, each once
- request_pages: int32 [4, 8, 4], replicated, may hold values from 0 to 255
Outputs:
- hidden_out: bfloat16 [2048, 4608], P(('dp', 'mp'))
- kv_new: bfloat16 [2048, 2, 32, 128], P('dp', None, 'mp')
Inputs may be any that keep to these rules, and one draw needn't show every extreme that they name: `key_value_weight`: query heads h and h2 with h // 2 == h2 // 2 have equal key and value weights: they share one key and value head. `key_value_cache`: query heads that share a key and value head have equal cached keys and values. `projected_lowrank_right`: the key and value parts of query heads that share a key and value head are equal. `token_request`: numbers never fall along a group; every request has at least one token. `adapter_position`: each slot once. `request_pages`: pages may repeat within and across requests.
All inputs are finite; a program needn't handle non-finite values.
Results may differ from a plain program's by a relative error of at most 0.035.
Values may be sent and summed in bfloat16 or wider, within the bound.
No kernel may reach another device: no remote copies, remote signals or barrier semaphores. Data moves between devices by JAX's collectives and lax.ppermute only.
A program may use at most 128 MiB of HBM per device.

v0:
```python
import math
import jax
import jax.numpy as jnp
from jax import lax
from jax.sharding import PartitionSpec as P

HIDDEN_BREADTH = 4608
ASKING_CHANNELS = 32
CHANNEL_LENGTH = 128
NUM_LOW_TERMS = 64
LOW_DIMENSION = 16
SHARD_PROMPTS = 8
PPR = 4
PAGE = 16
EPS = 1e-06
SOFTCAP = 50.0


def rms_scale(values, scaling):
    mean_square = jnp.mean(values * values, axis=-1, keepdims=True)
    return values * lax.rsqrt(mean_square + EPS) * scaling


def apply_rotary(values, token_positions):
    half_dim = values.shape[-1] // 2
    frequency = 10000.0 ** (-2.0 * jnp.arange(half_dim, dtype=jnp.float32) / values.shape[-1])
    angles = token_positions.astype(jnp.float32)[:, None] * frequency[None, :]
    cosine = jnp.cos(angles)[:, None, :]
    sine_part = jnp.sin(angles)[:, None, :]
    first_half = values[..., :half_dim]
    second_half = values[..., half_dim:]
    return jnp.concatenate(
        [
            first_half * cosine - second_half * sine_part,
            second_half * cosine + first_half * sine_part,
        ],
        axis=-1,
    )


def positions_of(segments):
    length = segments.shape[0]
    earlier = jnp.sum((segments[None, :] < segments[:, None]).astype(jnp.int32), axis=1)
    return PPR * PAGE + jnp.arange(length, dtype=jnp.int32) - earlier


def capped(scores):
    return SOFTCAP * jnp.tanh(scores / SOFTCAP)


def attend_local(query_rows, keys_new, fresh_values, keys_pre, values_pre, segments):
    scale_factor = 1.0 / math.sqrt(HIDDEN_BREADTH // ASKING_CHANNELS)
    length = segments.shape[0]
    prefix_owner = jnp.arange(keys_pre.shape[1], dtype=jnp.int32) // (PPR * PAGE)
    mask_pre = (prefix_owner[None, :] == segments[:, None])[None]
    ordinal = jnp.arange(length, dtype=jnp.int32)
    mask_new = ((segments[None, :] == segments[:, None]) & (ordinal[None, :] <= ordinal[:, None]))[
        None
    ]
    scores_pre = (
        jnp.einsum("thd,hjd->htj", query_rows, keys_pre, preferred_element_type=jnp.float32)
        * scale_factor
    )
    scores_new = (
        jnp.einsum("thd,uhd->htu", query_rows, keys_new, preferred_element_type=jnp.float32)
        * scale_factor
    )
    weight_pre = jnp.where(mask_pre, jnp.exp(capped(scores_pre)), 0.0)
    weight_new = jnp.where(mask_new, jnp.exp(capped(scores_new)), 0.0)
    totals = jnp.sum(weight_pre, axis=-1, keepdims=True) + jnp.sum(
        weight_new, axis=-1, keepdims=True
    )
    probs_pre = (weight_pre / totals).astype(jnp.bfloat16)
    probs_new = (weight_new / totals).astype(jnp.bfloat16)
    mixture = jnp.einsum("htj,hjd->thd", probs_pre, values_pre, preferred_element_type=jnp.float32)
    mixture = mixture + jnp.einsum(
        "htu,uhd->thd", probs_new, fresh_values, preferred_element_type=jnp.float32
    )
    return mixture.astype(jnp.bfloat16).reshape(length, -1)


def shards(
    residual_input,
    before_attention_gain,
    after_attention_gain,
    before_feedforward_gain,
    after_feedforward_gain,
    query_weight,
    key_value_weight,
    output_weight,
    gate_matrix,
    up_matrix,
    down_matrix,
    key_value_cache,
    projected_lowrank_left,
    projected_lowrank_right,
    result_lowrank_left,
    result_lowrank_right,
    token_request,
    lowrank_choice_by_prompt,
    adapter_position,
    request_pages,
):
    mp_index = lax.axis_index("mp")
    dp_index = lax.axis_index("dp")
    residual = residual_input.astype(jnp.float32)
    normed_rows = rms_scale(residual, before_attention_gain).astype(jnp.bfloat16)
    normalized_rows = lax.all_gather(normed_rows, "mp", axis=0, tiled=True)
    prompt_ordinal = normalized_rows.shape[0]
    channel_window = query_weight.shape[1] // CHANNEL_LENGTH
    query_rows = jnp.dot(normalized_rows, query_weight, preferred_element_type=jnp.float32).reshape(
        prompt_ordinal, channel_window, CHANNEL_LENGTH
    )
    key_value_rows = jnp.dot(
        normalized_rows,
        key_value_weight.reshape(HIDDEN_BREADTH, 2 * channel_window * CHANNEL_LENGTH),
        preferred_element_type=jnp.float32,
    ).reshape(prompt_ordinal, 2, channel_window, CHANNEL_LENGTH)
    segments = token_request[0]
    request_ids = lowrank_choice_by_prompt[0]
    request_range = jnp.arange(SHARD_PROMPTS, dtype=jnp.int32)
    membership = segments[:, None] == request_range[None, :]
    adapter_range = jnp.arange(NUM_LOW_TERMS, dtype=jnp.int32)
    token_adapter = jnp.sum(jnp.where(membership, request_ids[None, :], 0), axis=1)
    token_adapter_slot = jnp.sum(
        jnp.where(token_adapter[:, None] == adapter_range[None, :], adapter_position[None, :], 0),
        axis=1,
    )
    gathered_down = lax.all_gather(projected_lowrank_left, "mp", axis=0, tiled=True)
    request_slot = jnp.sum(
        jnp.where(request_ids[:, None] == adapter_range[None, :], adapter_position[None, :], 0),
        axis=1,
    )
    request_down = gathered_down[request_slot]
    request_factors = jnp.einsum(
        "td,rdk->trk", normalized_rows, request_down, preferred_element_type=jnp.float32
    )
    lowrank_source = jnp.sum(jnp.where(membership[:, :, None], request_factors, 0.0), axis=1)
    lowrank_source = lowrank_source.astype(jnp.bfloat16)
    choice_mask_table = membership.astype(jnp.bfloat16)
    broadened_lines = (choice_mask_table[:, :, None] * lowrank_source[:, None, :]).reshape(
        prompt_ordinal, SHARD_PROMPTS * LOW_DIMENSION
    )
    raised_result_lines = projected_lowrank_right[request_ids].reshape(
        SHARD_PROMPTS * LOW_DIMENSION, 3 * channel_window * CHANNEL_LENGTH
    )
    adapter_query_key_value = jnp.dot(
        broadened_lines, raised_result_lines, preferred_element_type=jnp.float32
    ).reshape(prompt_ordinal, 3, channel_window, CHANNEL_LENGTH)
    token_positions = positions_of(segments)
    rotary_queries = apply_rotary(
        query_rows + adapter_query_key_value[:, 0], token_positions
    ).astype(jnp.bfloat16)
    rotary_keys = apply_rotary(
        key_value_rows[:, 0] + adapter_query_key_value[:, 1], token_positions
    ).astype(jnp.bfloat16)
    fresh_values = (key_value_rows[:, 1] + adapter_query_key_value[:, 2]).astype(jnp.bfloat16)
    kv_new = jnp.stack([rotary_keys, fresh_values], axis=1)
    own_pages = lax.dynamic_index_in_dim(request_pages, dp_index, 0, keepdims=False).reshape(
        SHARD_PROMPTS * PPR
    )
    whole_pool = lax.all_gather(key_value_cache, "dp", axis=0, tiled=True)
    chosen = whole_pool[own_pages]
    keys_pre = jnp.transpose(chosen[:, 0], (1, 0, 2, 3)).reshape(
        channel_window, SHARD_PROMPTS * PPR * PAGE, CHANNEL_LENGTH
    )
    values_pre = jnp.transpose(chosen[:, 1], (1, 0, 2, 3)).reshape(
        channel_window, SHARD_PROMPTS * PPR * PAGE, CHANNEL_LENGTH
    )
    attended = attend_local(
        rotary_queries, rotary_keys, fresh_values, keys_pre, values_pre, segments
    )
    request_output_down = result_lowrank_left[request_ids]
    request_output_factors = jnp.einsum(
        "tc,rck->trk", attended, request_output_down, preferred_element_type=jnp.float32
    )
    output_adapter_piece = jnp.sum(
        jnp.where(membership[:, :, None], request_output_factors, 0.0), axis=1
    )
    result_lowrank_source = lax.psum(output_adapter_piece.astype(jnp.bfloat16), "mp")
    result_seat_lines = result_lowrank_right.shape[0]
    output_slots = mp_index * result_seat_lines + jnp.arange(result_seat_lines, dtype=jnp.int32)
    resident_here = (token_adapter_slot[:, None] == output_slots[None, :]).astype(jnp.bfloat16)
    broadened_result = (resident_here[:, :, None] * result_lowrank_source[:, None, :]).reshape(
        prompt_ordinal, result_seat_lines * LOW_DIMENSION
    )
    raised_window = result_lowrank_right.reshape(result_seat_lines * LOW_DIMENSION, HIDDEN_BREADTH)
    attn_sum = lax.psum_scatter(
        (
            jnp.dot(attended, output_weight, preferred_element_type=jnp.float32)
            + jnp.dot(broadened_result, raised_window, preferred_element_type=jnp.float32)
        ).astype(jnp.bfloat16),
        "mp",
        scatter_dimension=0,
        tiled=True,
    ).astype(jnp.float32)
    after_attn = (residual + rms_scale(attn_sum, after_attention_gain)).astype(jnp.bfloat16)
    normed_ffw = rms_scale(after_attn.astype(jnp.float32), before_feedforward_gain).astype(
        jnp.bfloat16
    )
    piece = lax.all_gather(normed_ffw, "mp", axis=0, tiled=True)
    gated = jnp.dot(piece, gate_matrix, preferred_element_type=jnp.float32)
    upward = jnp.dot(piece, up_matrix, preferred_element_type=jnp.float32)
    hidden = (jax.nn.gelu(gated, approximate=True) * upward).astype(jnp.bfloat16)
    ffw_sum = lax.psum_scatter(
        jnp.dot(hidden, down_matrix, preferred_element_type=jnp.float32).astype(jnp.bfloat16),
        "mp",
        scatter_dimension=0,
        tiled=True,
    ).astype(jnp.float32)
    hidden_out = (
        after_attn.astype(jnp.float32) + rms_scale(ffw_sum, after_feedforward_gain)
    ).astype(jnp.bfloat16)
    return (hidden_out, kv_new)


def solution(mesh):
    return jax.shard_map(
        shards,
        mesh=mesh,
        in_specs=(
            P(("dp", "mp"), None),
            P(),
            P(),
            P(),
            P(),
            P(None, "mp"),
            P(None, None, "mp", None),
            P("mp", None),
            P(None, "mp"),
            P(None, "mp"),
            P("mp", None),
            P("dp", None, "mp", None, None),
            P("mp", None, None),
            P(None, None, None, "mp", None),
            P(None, "mp", None),
            P("mp", None, None),
            P("dp", None),
            P("dp", None),
            P(),
            P(),
        ),
        out_specs=(P(("dp", "mp"), None), P("dp", None, "mp", None)),
        check_vma=False,
    )
```

profile of v0, /device:TPU:0, one launch (start us, length us, event | category | flops | bytes accessed | tf_op | source)
XLA Modules:
  0.0 1112.8 jit_solution(17951339612052338414)
XLA Ops:
  7.2 0.7 all-gather.5.cloned.1.call-update
  8.0 1.1 fusion.31
  9.0 1.7 fusion.33
  10.8 0.7 all-gather.9.cloned.1.call-update
  11.5 0.7 constant_dynamic-slice_fusion
  12.2 0.1 copy.46
  12.3 0.1 reshape.488
  12.4 0.7 fusion.73
  13.1 2.1 gather_fusion.3
  15.2 1.7 gather_fusion.2
  16.9 0.8 copy.48
  17.7 2.0 copy.60
  19.7 2.5 copy.50
  22.3 0.2 select_reduce_fusion.4
  22.5 0.1 select_reduce_fusion.3
  22.6 0.1 select_reduce_fusion.2
  22.7 0.2 convert_reduce_fusion
  23.0 15.9 %all-gather.5.cloned.1.call-done = bf16[256,2,1,16,128]{4,3,2,1,0:T(8,128)(2,1)} async-done(((bf16[64,2,1,16,128]{4,3,2,1,0:T(8,128)(2,1)}), bf16[256,2,1,16,128]{4,3,2,1,0:T(8,128)(2,1)}) %all-gather.5.cloned.1.call-update) | async-done | bytes 2097168 | tf_op jit(solution)/shard_map/all_gather | solution.py:162
  38.9 2.2 gather_fusion
  41.2 157.9 %all-gather.7.cloned.1.call-done = bf16[512,4608]{1,0:T(8,128)(2,1)} async-done(((bf16[16,4608]{1,0:T(8,128)(2,1)}), bf16[512,4608]{1,0:T(8,128)(2,1)}) %all-gather.7.cloned.1.call-update) | async-done | bytes 4718608 | tf_op jit(solution)/shard_map/all_gather | solution.py:108
  199.1 4.5 fusion.19
  203.6 207.7 %all-gather.9.cloned.1.call-done = bf16[64,4608,16]{1,2,0:T(8,128)(2,1)} async-done(((bf16[2,4608,16]{1,2,0:T(8,128)(2,1)}), bf16[64,4608,16]{1,2,0:T(8,128)(2,1)}) %all-gather.9.cloned.1.call-update) | async-done | bytes 9437200 | tf_op jit(solution)/shard_map/all_gather | solution.py:129
  411.2 4.3 gather_fusion.1
  415.6 4.1 fusion.84
  419.8 0.2 convolution_bitcast_fusion
  420.0 0.1 fusion.39
  420.1 1.7 fusion.22
  421.8 0.6 fusion.54
  422.4 0.5 fusion.82
  422.9 0.5 fusion.83
  423.4 0.3 fusion.26
  423.7 0.2 fusion.24
  423.9 0.2 fusion.86
  424.2 157.2 %psum.7 = bf16[512,16]{0,1:T(8,128)(2,1)S(1)} all-reduce(bf16[512,16]{0,1:T(8,128)(2,1)S(1)} %select_reduce_fusion), channel_id=1, replica_groups=mesh['dp'=4,'mp'=32] {'mp'}, use_global_device_ids=true, to_apply=%region_9.10 | all-reduce | flops 8192 | bytes 32768 | tf_op jit(solution)/shard_map/psum | solution.py:180
  581.4 1.4 fusion.63
  582.8 3.5 fusion
  586.4 165.2 %reduce-scatter.3.cloned.1.call-done = bf16[16,4608]{1,0:T(8,128)(2,1)} async-done(((bf16[512,4608]{1,0:T(8,128)(2,1)}), bf16[16,4608]{1,0:T(8,128)(2,1)}) %reduce-scatter.3.cloned.1.call-update) | async-done | bytes 147472 | tf_op jit(solution)/shard_map/reduce_scatter | solution.py:188
  751.6 1.1 fusion.27
  752.7 1.2 fusion.35
  753.9 0.8 fusion.37
  754.7 0.2 reduce-scatter.5.cloned.1.call-start
  754.9 154.9 %all-gather.11.cloned.1.call-done = bf16[512,4608]{1,0:T(8,128)(2,1)} async-done(((bf16[16,4608]{1,0:T(8,128)(2,1)}), bf16[512,4608]{1,0:T(8,128)(2,1)}) %all-gather.11.cloned.1.call-update) | async-done | bytes 4718608 | tf_op jit(solution)/shard_map/all_gather | solution.py:201
  909.8 7.4 fusion.85
  917.2 14.2 %convolution_convert_fusion = bf16[512,4608]{1,0:T(8,128)(2,1)} fusion(bf16[640,4608]{1,0:T(8,128)(2,1)} %param.30, bf16[512,4608]{1,0:T(8,128)(2,1)} %all-gather.11.cloned.1.call-done, bf16[4608,640]{1,0:T(8,128)(2,1)} %param.29, f32[512,640]{1,0:T(8,128)S(1)} %fusion.85), kind=kOutput, calls=%fused_computation.6 | convolution fusion | flops 6045433856 | bytes 22544384 | tf_op jit(solution)/shard_map/dot_general | solution.py:206
  931.5 0.9 copy.52
  932.4 170.8 %reduce-scatter.5.cloned.1.call-done = bf16[16,4608]{1,0:T(8,128)(2,1)} async-done(((bf16[512,4608]{1,0:T(8,128)(2,1)}), bf16[16,4608]{1,0:T(8,128)(2,1)}) %reduce-scatter.5.cloned.1.call-update) | async-done | bytes 147472 | tf_op jit(solution)/shard_map/reduce_scatter | solution.py:205
  1103.2 1.1 fusion.29
  1104.3 1.7 fusion.38
  (63 shorter events, 0.7 us)
Async XLA Ops:
  7.2 575.7 %copy-start = (bf16[128,4608]{1,0:T(8,128)(2,1)S(1)}, bf16[128,4608]{1,0:T(8,128)(2,1)}, u32[]{:S(2)}) copy-start(bf16[128,4608]{1,0:T(8,128)(2,1)} %param.27) | copy-start | bytes 3538948
  7.2 31.8 %all-gather.5.cloned.1.call-start = ((), (), s32[]{:S(2)}) async-start(), calls=%async_computation.2 | async-start | bytes 2621440 | tf_op jit(solution)/shard_map/all_gather | solution.py:162
  7.9 191.1 %all-gather.7.cloned.1.call-start = ((), (), s32[]{:S(2)}) async-start(), calls=%async_computation.3 | async-start | bytes 4866048 | tf_op jit(solution)/shard_map/all_gather | solution.py:108
  10.7 400.5 %all-gather.9.cloned.1.call-start = ((), (), s32[]{:S(2)}) async-start(), calls=%async_computation.4 | async-start | bytes 9732096 | tf_op jit(solution)/shard_map/all_gather | solution.py:129
  11.5 740.1 %reduce-scatter.3.cloned.1.call-start = ((), (), s32[]{:S(2)}) async-start(), calls=%async_computation.5 | async-start | bytes 4866048 | tf_op jit(solution)/shard_map/reduce_scatter | solution.py:188
  17.7 4.6 copy-start.11
  17.7 4.6 copy-start.12
  17.7 4.8 copy-start.7
  415.5 4.2 copy-start.5
  415.5 4.6 slice-start
  415.6 4.6 copy-start.4
  415.6 4.6 slice-start.1
  422.9 1.0 copy-start.2
  423.4 158.0 %copy-start.6 = (bf16[2,16,4608]{2,1,0:T(8,128)(2,1)S(1)}, bf16[2,16,4608]{2,1,0:T(8,128)(2,1)}, u32[]{:S(2)}) copy-start(bf16[2,16,4608]{2,1,0:T(8,128)(2,1)} %param.35) | copy-start | bytes 884740
  586.4 166.3 %copy-start.3 = (bf16[16,4608]{1,0:T(8,128)(2,1)S(1)}, bf16[16,4608]{1,0:T(8,128)(2,1)}, u32[]{:S(2)}) copy-start(bf16[16,4608]{1,0:T(8,128)(2,1)} %param.20) | copy-start | bytes 442372
  586.4 166.3 %copy-start.8 = (f32[4608]{0:T(1024)S(1)}, f32[4608]{0:T(1024)}, u32[]{:S(2)}) copy-start(f32[4608]{0:T(1024)} %param.22) | copy-start | bytes 55300
  586.4 167.5 %copy-start.9 = (f32[4608]{0:T(1024)S(1)}, f32[4608]{0:T(1024)}, u32[]{:S(2)}) copy-start(f32[4608]{0:T(1024)} %param.23) | copy-start | bytes 55300
  586.4 323.4 %all-gather.11.cloned.1.call-start = ((), (), s32[]{:S(2)}) async-start(), calls=%async_computation.6 | async-start | bytes 4866048 | tf_op jit(solution)/shard_map/all_gather | solution.py:201
  754.7 348.5 %reduce-scatter.5.cloned.1.call-start = ((), (), s32[]{:S(2)}) async-start(), calls=%async_computation.7 | async-start | bytes 4866048 | tf_op jit(solution)/shard_map/reduce_scatter | solution.py:205
  917.2 188.7 %copy-start.1 = (bf16[128,4608]{1,0:T(8,128)(2,1)S(1)}, bf16[128,4608]{1,0:T(8,128)(2,1)}, u32[]{:S(2)}) copy-start(bf16[128,4608]{1,0:T(8,128)(2,1)} %param.27) | copy-start | bytes 3538948
  931.5 172.8 %copy-start.10 = (f32[4608]{0:T(1024)S(1)}, f32[4608]{0:T(1024)}, u32[]{:S(2)}) copy-start(f32[4608]{0:T(1024)} %param.24) | copy-start | bytes 55300
Sparse Core Ops, SparseCore 0:
  9.7 29.2 all-gather.4
  41.1 157.8 all-gather.6
  200.7 210.4 all-gather.8
  586.5 165.0 reduce-scatter.2
  754.8 154.9 all-gather.10
  931.6 171.5 reduce-scatter.4
where the time goes:
time: 1110 us
  waiting for transfers between devices  874 us (79%)
  blocking collectives  157 us (14%)
  matrix products  38.8 us (3%)
  local copies, waits for them, and re-layouts  17.5 us (2%)
  between operations  14.5 us (1%)
    all_gather x1, waiting for transfers between devices, shards(): lax.all_gather(projected_lowrank_left, 'mp', axis=0, tiled=True)  208 us
    reduce_scatter x1, waiting for transfers between devices, shards(): lax.psum_scatter(jnp.dot(hidden, down_matrix, preferred_element_type=jnp....  171 us
    reduce_scatter x1, waiting for transfers between devices, shards(): lax.psum_scatter((jnp.dot(attended, output_weight, preferred_element_type...  165 us
    all_gather x1, waiting for transfers between devices, shards(): normalized_rows = lax.all_gather(normed_rows, 'mp', axis=0, tiled=True)  158 us
    psum x1, blocking collectives, shards(): lax.psum(output_adapter_piece.astype(jnp.bfloat16), 'mp')  157 us
    all_gather x1, waiting for transfers between devices, shards(): piece = lax.all_gather(normed_ffw, 'mp', axis=0, tiled=True)  155 us
  transfers between devices with their start and end apart: 6, of which 6 were waited for; matrix products, arithmetic and copies ran while one was open for 2% of the time, Pallas kernels for 0%

commit v1 on v0

--- a/solution.py
+++ b/solution.py
@@ -105,7 +105,9 @@
     dp_index = lax.axis_index("dp")
     residual = residual_input.astype(jnp.float32)
     normed_rows = rms_scale(residual, before_attention_gain).astype(jnp.bfloat16)
-    normalized_rows = lax.all_gather(normed_rows, "mp", axis=0, tiled=True)
+    normalized_rows = jnp.concatenate(
+        lax.all_to_all(jnp.stack([normed_rows] * lax.axis_size("mp")), "mp", 0, 0), axis=0
+    )
     prompt_ordinal = normalized_rows.shape[0]
     channel_window = query_weight.shape[1] // CHANNEL_LENGTH
     query_rows = jnp.dot(normalized_rows, query_weight, preferred_element_type=jnp.float32).reshape(

time: 1110 us -> 1000 us (0.901)
  waiting for transfers between devices: 874 us -> 754 us
    all_gather x1 -> x0, waiting for transfers between devices: 158 us -> none  [shards(): normalized_rows = lax.all_gather(normed_rows, 'mp', axis=0, tiled=True)]
    all_gather x1, waiting for transfers between devices: 15.9 us -> 54.7 us  [shards(): whole_pool = lax.all_gather(key_value_cache, 'dp', axis=0, tiled=True)]
where the time goes in v1:
time: 1000 us
  waiting for transfers between devices  754 us (75%)
  blocking collectives  157 us (16%)
  matrix products  41.2 us (4%)
  local copies, waits for them, and re-layouts  19.2 us (2%)
  between operations  14.1 us (1%)
    all_gather x1, waiting for transfers between devices, shards(): lax.all_gather(projected_lowrank_left, 'mp', axis=0, tiled=True)  200 us
    reduce_scatter x1, waiting for transfers between devices, shards(): lax.psum_scatter(jnp.dot(hidden, down_matrix, preferred_element_type=jnp....  171 us
    reduce_scatter x1, waiting for transfers between devices, shards(): lax.psum_scatter((jnp.dot(attended, output_weight, preferred_element_type...  166 us
    psum x1, blocking collectives, shards(): lax.psum(output_adapter_piece.astype(jnp.bfloat16), 'mp')  157 us
    all_gather x1, waiting for transfers between devices, shards(): piece = lax.all_gather(normed_ffw, 'mp', axis=0, tiled=True)  155 us
    all_gather x1, waiting for transfers between devices, shards(): whole_pool = lax.all_gather(key_value_cache, 'dp', axis=0, tiled=True)  54.7 us
  transfers between devices with their start and end apart: 6, of which 6 were waited for; matrix products, arithmetic and copies ran while one was open for 2% of the time, Pallas kernels for 0%

profile of v1, /device:TPU:0, one launch (start us, length us, event | category | flops | bytes accessed | tf_op | source)
XLA Modules:
  0.0 1004.3 jit_solution(13509973199017390004)
XLA Ops:
  7.2 0.7 all-gather.4.cloned.1.call-update
  8.0 0.7 all-gather.6.cloned.1.call-update
  8.7 1.1 fusion.26
  9.7 1.0 fusion.28
  10.8 2.7 stack.4
  13.4 9.0 all-to-all-start
  22.5 0.7 constant_dynamic-slice_fusion
  23.2 0.1 copy.46
  23.4 1.2 gather_fusion.3
  24.6 1.7 gather_fusion.2
  26.4 0.8 copy.48
  27.1 2.0 copy.60
  29.1 2.5 copy.50
  31.7 0.2 select_reduce_fusion.4
  31.9 0.1 select_reduce_fusion.3
  32.0 0.1 select_reduce_fusion.2
  32.1 0.2 convert_reduce_fusion
  32.4 54.7 %all-gather.4.cloned.1.call-done = bf16[256,2,1,16,128]{4,3,2,1,0:T(8,128)(2,1)} async-done(((bf16[64,2,1,16,128]{4,3,2,1,0:T(8,128)(2,1)}), bf16[256,2,1,16,128]{4,3,2,1,0:T(8,128)(2,1)}) %all-gather.4.cloned.1.call-update) | async-done | bytes 2097168 | tf_op jit(solution)/shard_map/all_gather | solution.py:164
  87.1 2.2 gather_fusion
  89.3 7.0 all-to-all-done
  96.2 4.6 convolution_bitcast_fusion.1
  100.9 199.7 %all-gather.6.cloned.1.call-done = bf16[64,4608,16]{1,2,0:T(8,128)(2,1)} async-done(((bf16[2,4608,16]{1,2,0:T(8,128)(2,1)}), bf16[64,4608,16]{1,2,0:T(8,128)(2,1)}) %all-gather.6.cloned.1.call-update) | async-done | bytes 9437200 | tf_op jit(solution)/shard_map/all_gather | solution.py:131
  300.6 4.3 gather_fusion.1
  304.9 4.1 fusion.79
  309.0 0.2 convolution_bitcast_fusion
  309.3 4.0 fusion.17
  313.3 0.1 fusion.34
  313.4 0.6 fusion.49
  314.0 0.5 fusion.77
  314.5 0.5 fusion.78
  315.0 0.3 fusion.21
  315.2 0.2 fusion.19
  315.5 0.2 fusion.81
  315.7 157.2 %psum.7 = bf16[512,16]{0,1:T(8,128)(2,1)S(1)} all-reduce(bf16[512,16]{0,1:T(8,128)(2,1)S(1)} %select_reduce_fusion), channel_id=1, replica_groups=mesh['dp'=4,'mp'=32] {'mp'}, use_global_device_ids=true, to_apply=%region_9.10 | all-reduce | flops 8192 | bytes 32768 | tf_op jit(solution)/shard_map/psum | solution.py:182
  473.0 1.4 fusion.58
  474.4 3.5 fusion
  478.0 165.5 %reduce-scatter.3.cloned.1.call-done = bf16[16,4608]{1,0:T(8,128)(2,1)} async-done(((bf16[512,4608]{1,0:T(8,128)(2,1)}), bf16[16,4608]{1,0:T(8,128)(2,1)}) %reduce-scatter.3.cloned.1.call-update) | async-done | bytes 147472 | tf_op jit(solution)/shard_map/reduce_scatter | solution.py:190
  643.5 1.1 fusion.22
  644.6 1.2 fusion.30
  645.8 0.8 fusion.32
  646.6 0.2 reduce-scatter.5.cloned.1.call-start
  646.8 154.7 %all-gather.8.cloned.1.call-done = bf16[512,4608]{1,0:T(8,128)(2,1)} async-done(((bf16[16,4608]{1,0:T(8,128)(2,1)}), bf16[512,4608]{1,0:T(8,128)(2,1)}) %all-gather.8.cloned.1.call-update) | async-done | bytes 4718608 | tf_op jit(solution)/shard_map/all_gather | solution.py:203
  801.5 7.4 fusion.80
  808.9 14.2 %convolution_convert_fusion = bf16[512,4608]{1,0:T(8,128)(2,1)} fusion(bf16[640,4608]{1,0:T(8,128)(2,1)} %param.30, bf16[512,4608]{1,0:T(8,128)(2,1)} %all-gather.8.cloned.1.call-done, bf16[4608,640]{1,0:T(8,128)(2,1)} %param.29, f32[512,640]{1,0:T(8,128)S(1)} %fusion.80), kind=kOutput, calls=%fused_computation.6 | convolution fusion | flops 6045433856 | bytes 22544384 | tf_op jit(solution)/shard_map/dot_general | solution.py:208
  823.2 0.9 copy.52
  824.1 170.9 %reduce-scatter.5.cloned.1.call-done = bf16[16,4608]{1,0:T(8,128)(2,1)} async-done(((bf16[512,4608]{1,0:T(8,128)(2,1)}), bf16[16,4608]{1,0:T(8,128)(2,1)}) %reduce-scatter.5.cloned.1.call-update) | async-done | bytes 147472 | tf_op jit(solution)/shard_map/reduce_scatter | solution.py:207
  995.0 1.1 fusion.24
  996.1 1.7 fusion.33
  (60 shorter events, 0.7 us)
Async XLA Ops:
  7.2 467.2 %copy-start = (bf16[128,4608]{1,0:T(8,128)(2,1)S(1)}, bf16[128,4608]{1,0:T(8,128)(2,1)}, u32[]{:S(2)}) copy-start(bf16[128,4608]{1,0:T(8,128)(2,1)} %param.27) | copy-start | bytes 3538948
  7.2 79.9 %all-gather.4.cloned.1.call-start = ((), (), s32[]{:S(2)}) async-start(), calls=%async_computation.3 | async-start | bytes 2621440 | tf_op jit(solution)/shard_map/all_gather | solution.py:164
  7.9 292.6 %all-gather.6.cloned.1.call-start = ((), (), s32[]{:S(2)}) async-start(), calls=%async_computation.4 | async-start | bytes 9732096 | tf_op jit(solution)/shard_map/all_gather | solution.py:131
  13.4 10.0 copy-start.12
  13.4 10.0 copy-start.7
  13.4 82.8 %all-to-all-start = ((bf16[32,16,4608]{2,1,0:T(8,128)(2,1)}), bf16[32,16,4608]{2,1,0:T(8,128)(2,1)}, u32[]{:S(2)}, u32[]{:S(2)}) async-start(bf16[32,16,4608]{2,1,0:T(8,128)(2,1)} %stack.4), calls=%async_computation | async-start | bytes 9437184 | tf_op jit(solution)/shard_map/all_to_all | solution.py:109
  22.5 621.0 %reduce-scatter.3.cloned.1.call-start = ((), (), s32[]{:S(2)}) async-start(), calls=%async_computation.5 | async-start | bytes 4866048 | tf_op jit(solution)/shard_map/reduce_scatter | solution.py:190
  27.1 4.6 copy-start.13
  27.1 4.8 copy-start.8
  304.9 4.2 copy-start.5
  304.9 4.4 copy-start.4
  314.5 1.0 copy-start.2
  315.0 158.0 %copy-start.6 = (bf16[2,16,4608]{2,1,0:T(8,128)(2,1)S(1)}, bf16[2,16,4608]{2,1,0:T(8,128)(2,1)}, u32[]{:S(2)}) copy-start(bf16[2,16,4608]{2,1,0:T(8,128)(2,1)} %param.35) | copy-start | bytes 884740
  477.9 166.7 %copy-start.3 = (bf16[16,4608]{1,0:T(8,128)(2,1)S(1)}, bf16[16,4608]{1,0:T(8,128)(2,1)}, u32[]{:S(2)}) copy-start(bf16[16,4608]{1,0:T(8,128)(2,1)} %param.20) | copy-start | bytes 442372
  477.9 166.7 %copy-start.9 = (f32[4608]{0:T(1024)S(1)}, f32[4608]{0:T(1024)}, u32[]{:S(2)}) copy-start(f32[4608]{0:T(1024)} %param.22) | copy-start | bytes 55300
  477.9 167.8 %copy-start.10 = (f32[4608]{0:T(1024)S(1)}, f32[4608]{0:T(1024)}, u32[]{:S(2)}) copy-start(f32[4608]{0:T(1024)} %param.23) | copy-start | bytes 55300
  478.0 323.5 %all-gather.8.cloned.1.call-start = ((), (), s32[]{:S(2)}) async-start(), calls=%async_computation.6 | async-start | bytes 4866048 | tf_op jit(solution)/shard_map/all_gather | solution.py:203
  646.6 348.4 %reduce-scatter.5.cloned.1.call-start = ((), (), s32[]{:S(2)}) async-start(), calls=%async_computation.7 | async-start | bytes 4866048 | tf_op jit(solution)/shard_map/reduce_scatter | solution.py:207
  808.9 188.9 %copy-start.1 = (bf16[128,4608]{1,0:T(8,128)(2,1)S(1)}, bf16[128,4608]{1,0:T(8,128)(2,1)}, u32[]{:S(2)}) copy-start(bf16[128,4608]{1,0:T(8,128)(2,1)} %param.27) | copy-start | bytes 3538948
  823.2 172.9 %copy-start.11 = (f32[4608]{0:T(1024)S(1)}, f32[4608]{0:T(1024)}, u32[]{:S(2)}) copy-start(f32[4608]{0:T(1024)} %param.24) | copy-start | bytes 55300
Sparse Core Ops, SparseCore 0:
  9.7 77.3 all-gather.3
  88.7 211.8 all-gather.5
  478.1 165.3 reduce-scatter.2
  646.7 154.7 all-gather.7
  823.3 171.6 reduce-scatter.4
